TPU v7x, 256 devices: a whole 4x4x8 slice. The times are simulated.
256 devices in a mesh: row: 16 (over z, y_hi), col: 16 (over x, y_lo, core).
Axes of the slice: x: 4, y: 4 (y_hi: 2, y_lo: 2; y = y_hi * 2 + y_lo), z: 8, core: 2. Of those that a mesh axis runs over, the one named last changes fastest.
Arguments:
- features: bfloat16 [512, 512, 256], P('row', 'col'), may hold values from -6 to 6
- dw_kernel: bfloat16 [7, 7, 256], replicated, may hold values from -0.875 to 0.875
- dw_bias: float32 [256], replicated, may hold values from -4 to 4
- norm_gain: float32 [256], replicated, may hold values from 0.5 to 2
- norm_bias: float32 [256], replicated, may hold values from -3 to 3
- w_expand: bfloat16 [256, 1024], replicated, may hold values from -0.375 to 0.375
- b_expand: float32 [1024], replicated, may hold values from -3 to 3
- w_reduce: bfloat16 [1024, 256], replicated, may hold values from -0.1875 to 0.1875
- b_reduce: float32 [256], replicated, may hold values from -3 to 3
- layer_scale: float32 [256], replicated, may hold values from 0.5 to 2
- w_query: bfloat16 [256, 256], replicated, may hold values from -2 to 2
- w_keyval: bfloat16 [256, 512], replicated, may hold values from -0.375 to 0.375
- rel_bias: float32 [8, 7, 127], replicated, may hold values from -8 to 250, as said below
- w_out: bfloat16 [256, 256], replicated, may hold values from -0.75 to 0.75
Outputs:
- result: bfloat16 [512, 512, 256], P('row', 'col')
Inputs may be any that keep to these rules, and one draw needn't show every extreme that they name: `rel_bias`: relative position bias of moderate size, with possibly a few much larger entries.
All inputs are finite; a program needn't handle non-finite values.
Results may differ from a plain program's by a relative error of at most 0.014.
Values may be sent and summed in bfloat16 or wider, within the bound.
No kernel may reach another device: no remote copies, remote signals or barrier semaphores. Data moves between devices by JAX's collectives and lax.ppermute only.
A program may use at most 64 MiB of HBM per device.

v0:
```python
import jax
import jax.numpy as jnp
from jax import lax
from jax.sharding import PartitionSpec as P

HEADS = 8


def padded_2(array, sides, width):
    for axis, dim in sides:
        devices, length = (lax.axis_size(axis), array.shape[dim])
        up = [(i, (i + 1) % devices) for i in range(devices - 1)]
        down = [(j, i) for i, j in up]
        last = lax.slice_in_dim(array, length - width, length, axis=dim)
        leading = lax.slice_in_dim(array, 0, width, axis=dim)
        before = lax.ppermute(last, axis, up)
        after = lax.ppermute(leading, axis, down)
        array = jnp.concatenate([before, array, after], axis=dim)
    return array


def block_pass(
    padded,
    features,
    dw_kernel,
    dw_bias,
    norm_gain,
    norm_bias,
    w_expand,
    b_expand,
    w_reduce,
    b_reduce,
    layer_scale,
):
    tile_rows, tile_cols, channels = features.shape
    convolved = jnp.zeros((tile_rows, tile_cols, channels), jnp.float32)
    for tap_row in range(7):
        for tap_col in range(7):
            convolved = convolved + padded[
                tap_row : tap_row + tile_rows, tap_col : tap_col + tile_cols
            ].astype(jnp.float32) * dw_kernel[tap_row, tap_col].astype(jnp.float32)
    convolved = convolved + dw_bias
    average = jnp.mean(convolved, axis=-1, keepdims=True)
    centred = convolved - average
    variance = jnp.mean(centred * centred, axis=-1, keepdims=True)
    normed = (
        (centred * lax.rsqrt(variance + 1e-06) * norm_gain + norm_bias)
        .astype(jnp.bfloat16)
        .reshape(-1, channels)
    )
    hidden = jax.nn.gelu(
        jnp.dot(normed, w_expand, preferred_element_type=jnp.float32) + b_expand, approximate=False
    ).astype(jnp.bfloat16)
    reduced = jnp.dot(hidden, w_reduce, preferred_element_type=jnp.float32) + b_reduce
    summed = features.astype(jnp.float32).reshape(-1, channels) + layer_scale * reduced
    return summed.astype(jnp.bfloat16).reshape(tile_rows, tile_cols, channels)


def shards(
    features,
    dw_kernel,
    dw_bias,
    norm_gain,
    norm_bias,
    w_expand,
    b_expand,
    w_reduce,
    b_reduce,
    layer_scale,
    w_query,
    w_keyval,
    rel_bias,
    w_out,
):
    tile_rows, tile_cols, channels = features.shape
    head_dim = channels // HEADS
    extended = padded_2(features, (("row", 0),), 3)
    padded = padded_2(extended, (("col", 1),), 3)
    block_out = block_pass(
        padded,
        features,
        dw_kernel,
        dw_bias,
        norm_gain,
        norm_bias,
        w_expand,
        b_expand,
        w_reduce,
        b_reduce,
        layer_scale,
    )
    region_side = tile_rows // 8
    local_count = region_side * region_side
    pooled = (
        block_out.astype(jnp.float32)
        .reshape(region_side, 8, region_side, 8, channels)
        .mean(axis=(1, 3))
    )
    pooled = pooled.astype(jnp.bfloat16).reshape(local_count, channels)
    queries = jnp.dot(pooled, w_query, preferred_element_type=jnp.float32).astype(jnp.bfloat16)
    keyval = jnp.dot(pooled, w_keyval, preferred_element_type=jnp.float32).astype(jnp.bfloat16)
    band_keyval = lax.all_gather(keyval, "col", axis=0, tiled=True)
    columns = lax.axis_size("col")
    position = lax.axis_index("col")
    span_cols = region_side * columns
    key_count = local_count * columns
    side_index = jnp.arange(region_side, dtype=jnp.int32)
    row_offsets = side_index[None, :] - side_index[:, None] + region_side - 1
    row_onehot = (
        row_offsets[:, :, None] == jnp.arange(2 * region_side - 1, dtype=jnp.int32)[None, None, :]
    ).astype(jnp.float32)
    row_picked = jnp.einsum("rso,hoc->hrsc", row_onehot, rel_bias, precision=lax.Precision.HIGHEST)
    query_cols = position * region_side + side_index
    span_index = jnp.arange(span_cols, dtype=jnp.int32)
    col_offsets = span_index[None, :] - query_cols[:, None] + span_cols - 1
    col_onehot = (
        col_offsets[:, :, None] == jnp.arange(2 * span_cols - 1, dtype=jnp.int32)[None, None, :]
    ).astype(jnp.float32)
    both_picked = jnp.einsum(
        "hrsc,qkc->hrqsk", row_picked, col_onehot, precision=lax.Precision.HIGHEST
    )
    both_picked = both_picked.reshape(
        HEADS, region_side, region_side, region_side, columns, region_side
    )
    bias_block = jnp.transpose(both_picked, (0, 1, 2, 4, 3, 5)).reshape(
        HEADS, local_count, key_count
    )
    query_heads = queries.reshape(local_count, HEADS, head_dim)
    key_heads = band_keyval[:, :channels].reshape(key_count, HEADS, head_dim)
    value_heads = band_keyval[:, channels:].reshape(key_count, HEADS, head_dim)
    scores = (
        jnp.einsum("qhd,khd->hqk", query_heads, key_heads, preferred_element_type=jnp.float32)
        / jnp.sqrt(jnp.float32(head_dim))
        + bias_block
    )
    attn = jax.nn.softmax(scores, axis=-1).astype(jnp.bfloat16)
    context = (
        jnp.einsum("hqk,khd->qhd", attn, value_heads, preferred_element_type=jnp.float32)
        .reshape(local_count, channels)
        .astype(jnp.bfloat16)
    )
    lifted = jnp.dot(context, w_out, preferred_element_type=jnp.float32).reshape(
        region_side, 1, region_side, 1, channels
    )
    spread = jnp.broadcast_to(lifted, (region_side, 8, region_side, 8, channels)).reshape(
        tile_rows, tile_cols, channels
    )
    return (block_out.astype(jnp.float32) + spread).astype(jnp.bfloat16)


def solution(mesh):
    return jax.shard_map(
        shards,
        mesh=mesh,
        in_specs=(
            P("row", "col", None),
            P(),
            P(),
            P(),
            P(),
            P(),
            P(),
            P(),
            P(),
            P(),
            P(),
            P(),
            P(),
            P(),
        ),
        out_specs=P("row", "col", None),
        check_vma=False,
    )
```

profile of v0, /device:TPU:129, one launch (start us, length us, event | category | flops | bytes accessed | tf_op | source)
XLA Modules:
  0.0 78.3 jit_solution(13312583361902755873)
XLA Ops:
  0.0 0.9 %fusion.106 = (bf16[3,32,256]{2,1,0:T(8,128)(2,1)S(1)}, bf16[3,32,256]{2,1,0:T(8,128)(2,1)S(1)}) fusion(bf16[32,32,256]{2,1,0:T(8,128)(2,1)} %param.14), kind=kLoop, calls=%fused_computation.266 | loop fusion | bytes 196608 | tf_op jit(solution)/shard_map/slice | solution.py:15
  0.9 4.8 %collective-permute-start = (bf16[3,32,256]{2,1,0:T(8,128)(2,1)S(1)}, bf16[3,32,256]{2,1,0:T(8,128)(2,1)S(1)}, u32[]{:S(2)}, u32[]{:S(2)}) collective-permute-start(bf16[3,32,256]{2,1,0:T(8,128)(2,1)S(1)} %get-tuple-element.13), channel_id=1, source_target_pairs={{0,16},{16,32},{32,48},{48,64},{64,80},{80,96},{96,112},{112,128},... | collective-permute-start | bytes 147464 | tf_op jit(solution)/shard_map/ppermute | solution.py:16
  5.7 4.1 %collective-permute-start.1 = (bf16[3,32,256]{2,1,0:T(8,128)(2,1)S(1)}, bf16[3,32,256]{2,1,0:T(8,128)(2,1)S(1)}, u32[]{:S(2)}, u32[]{:S(2)}) collective-permute-start(bf16[3,32,256]{2,1,0:T(8,128)(2,1)S(1)} %get-tuple-element.12), channel_id=1, source_target_pairs={{16,0},{32,16},{48,32},{64,48},{80,64},{96,80},{112,96},{128,112},... | collective-permute-start | bytes 147464 | tf_op jit(solution)/shard_map/ppermute | solution.py:17
  9.8 1.6 %slice_convert_fusion.48 = (f32[1,1,256]{2,1,0:T(1,128)S(1)}, f32[1,1,256]{2,1,0:T(1,128)S(1)}, f32[1,1,256]{2,1,0:T(1,128)S(1)}, f32[1,1,256]{2,1,0:T(1,128)S(1...) fusion(bf16[7,7,256]{2,1,0:T(8,128)(2,1)} %param.15), kind=kLoop, calls=%fused_computation.231 | loop fusion | flops 4864 | bytes 29184 | tf_op jit(solution)/shard_map/mul | solution.py:39
  11.4 0.1 subtract_add_fusion.1
  11.5 1.0 %fusion.67 = f32[4,4,8,127]{3,1,2,0:T(4,128)S(1)} fusion(f32[8,7,127,1]{2,0,1,3:T(8,128)} %bitcast.105, s32[4,4]{1,0:T(4,128)S(1)} %subtract_add_fusion), kind=kOutput, calls=%fused_computation.165 | convolution fusion | flops 1365616 | bytes 93536 | tf_op jit(solution)/shard_map/rso,hoc->hrsc/dot_general | solution.py:112
  12.5 0.4 convolution_bitcast_fusion
  12.9 1.7 %slice_convert_fusion.47 = (f32[1,1,256]{2,1,0:T(1,128)}, f32[1,1,256]{2,1,0:T(1,128)}, f32[1,1,256]{2,1,0:T(1,128)}, f32[1,1,256]{2,1,0:T(1,128)}, f32[1,1,256]...) fusion(bf16[7,7,256]{2,1,0:T(8,128)(2,1)} %param.15), kind=kLoop, calls=%fused_computation.230 | loop fusion | flops 4864 | bytes 29184 | tf_op jit(solution)/shard_map/mul | solution.py:39
  14.6 0.0 collective-permute-done
  14.6 1.2 %constant_dynamic-update-slice_fusion.3 = (bf16[35,32,256]{2,1,0:T(8,128)(2,1)S(1)}, bf16[38,32,256]{2,1,0:T(8,128)(2,1)S(1)}, bf16[35,32,256]{2,1,0:T(8,128)(2,1)S(1)}) fusion(bf16[35,32,256]{2,1,0:T(8,128)(2,1)S(1)} %get-tuple-element.16, bf16[32,32,256]{2,1,0:T(8,128)(2,1)} %param.14, bf16[38,32,256]{2,1,0:T(8,128)(2,1)S(1)} %get-tuple-element.17), kind=kLoop, calls=%fused_computation.171 | loop fusion | bytes 2097152 | tf_op jit(solution)/shard_map/concatenate | solution.py:18
  15.9 0.0 collective-permute-done.1
  15.9 0.9 %fusion.105 = (bf16[38,3,256]{2,1,0:T(4,128)(2,1)}, bf16[38,3,256]{2,1,0:T(4,128)(2,1)}) fusion(bf16[38,32,256]{2,1,0:T(8,128)(2,1)S(1)} %get-tuple-element.19), kind=kLoop, calls=%fused_computation.265 | loop fusion | bytes 233472 | tf_op jit(solution)/shard_map/slice | solution.py:14
  16.8 3.1 %collective-permute-start.3 = (bf16[38,3,256]{2,1,0:T(4,128)(2,1)}, bf16[38,3,256]{2,1,0:T(4,128)(2,1)S(1)}, u32[]{:S(2)}, u32[]{:S(2)}) collective-permute-start(bf16[38,3,256]{2,1,0:T(4,128)(2,1)} %get-tuple-element.8), channel_id=1, source_target_pairs={{1,0},{2,1},{3,2},{4,3},{5,4},{6,5},{7,6},{8,7},{9,8},{10,9},{11,1... | collective-permute-start | bytes 175112 | tf_op jit(solution)/shard_map/ppermute | solution.py:17
  19.9 3.1 %collective-permute-start.2 = (bf16[38,3,256]{2,1,0:T(4,128)(2,1)}, bf16[38,3,256]{2,1,0:T(4,128)(2,1)}, u32[]{:S(2)}, u32[]{:S(2)}) collective-permute-start(bf16[38,3,256]{2,1,0:T(4,128)(2,1)} %get-tuple-element.7), channel_id=1, source_target_pairs={{0,1},{1,2},{2,3},{3,4},{4,5},{5,6},{6,7},{7,8},{8,9},{9,10},{10,1... | collective-permute-start | bytes 175112 | tf_op jit(solution)/shard_map/ppermute | solution.py:16
  23.0 1.5 %slice_convert_fusion.46 = (f32[1,1,256]{2,1,0:T(1,128)}, f32[1,1,256]{2,1,0:T(1,128)}, f32[1,1,256]{2,1,0:T(1,128)}, f32[1,1,256]{2,1,0:T(1,128)}, f32[1,1,256]...) fusion(bf16[7,7,256]{2,1,0:T(8,128)(2,1)} %param.15), kind=kLoop, calls=%fused_computation.229 | loop fusion | flops 2816 | bytes 16896 | tf_op jit(solution)/shard_map/mul | solution.py:39
  24.5 0.6 copy.22
  25.1 1.8 %copy.23 = f32[8,4,4,16,4,4]{0,5,4,3,2,1:T(4,128)} copy(f32[8,4,4,16,4,4]{0,5,3,4,2,1:T(4,128)S(1)} %bitcast.96) | data formatting | bytes 262144 | tf_op jit(solution)/shard_map/transpose | solution.py:125
  27.3 2.5 %copy.24 = f32[8,16,256]{2,1,0:T(8,128)S(1)} copy(f32[8,16,256]{0,2,1:T(8,128)} %bitcast.97) | data formatting | bytes 262144 | tf_op jit(solution)/shard_map/reshape | solution.py:125
  29.7 0.0 collective-permute-done.3
  29.8 0.0 collective-permute-done.2
  29.8 0.0 copy-done.2
  29.8 0.0 copy-done.3
  29.8 0.0 copy-done.5
  29.8 0.0 copy-done.9
  29.8 0.0 copy-done.10
  29.8 0.0 copy-done.11
  29.8 0.0 copy-done.12
  29.8 0.0 copy-done.13
  29.8 0.0 copy-done.14
  29.9 0.0 copy-done.15
  29.9 0.0 copy-done.16
  29.9 0.0 copy-done.17
  29.9 0.0 copy-done.18
  29.9 0.0 copy-done.19
  29.9 0.0 copy-done.20
  29.9 0.0 copy-done.21
  29.9 0.0 copy-done.22
  29.9 0.0 copy-done.23
  29.9 0.0 copy-done.24
  30.0 0.0 copy-done.25
  30.2 13.4 %fusion.104 = (f32[32,32]{1,0:T(8,128)S(1)}, f32[32,32,256]{2,1,0:T(8,128)S(1)}) fusion(f32[256]{0:T(256)} %param.16, f32[256]{0:T(256)} %bitcast.153, bf16[38,3,256]{2,1,0:T(4,128)(2,1)S(1)} %collective-permute-done.3, bf16[38,32,256]{2,1,0:T(8,128)(2,1)S(1)} %copy-done.5, f32[256]{0:T(256)} %bitcast.154, f32[256]{0:T(256)S(1)} %bitcast.107, ...), kind=kLoop, calls=%fused_computation.264 | loop fusion | flops 71826432 | bytes 5513216 | tf_op jit(solution)/shard_map/reduce_sum | solution.py:43
  43.5 0.0 copy-start.45
  43.6 0.0 copy-start.46
  43.6 0.0 copy-start.47
  43.6 0.4 multiply_reduce_fusion
  44.0 1.0 %add_convert_fusion.1 = bf16[32,32,256]{2,1,0:T(8,128)(2,1)S(1)} fusion(f32[32,32,256]{2,1,0:T(8,128)S(1)} %get-tuple-element.6, f32[256]{0:T(256)} %param.18, f32[256]{0:T(256)} %param.17, f32[32,32]{1,0:T(8,128)S(1)} %add_rsqrt_fusion, f32[32,32]{1,0:T(8,128)S(1)} %broadcast_multiply_fusion), kind=kLoop, calls=%fused_computation.75 | loop fusion | flops 1310720 | bytes 1583104 | tf_op jit(solution)/shard_map/convert_element_type | solution.py:48
  45.1 0.0 copy-start.6
  45.1 10.9 %fusion.14 = f32[1024,256]{1,0:T(8,128)S(1)} fusion(bf16[1024,256]{1,0:T(8,128)(2,1)S(1)} %copy-done, bf16[1024,256]{1,0:T(8,128)(2,1)S(1)} %bitcast.102, bf16[256,1024]{1,0:T(8,128)(2,1)} %param.19, f32[1024]{0:T(1024)S(1)} %copy-done.45, f32[256]{0:T(256)S(1)} %copy-done.46, f32[256]{0:T(256)S(1)} %copy-done.47, bf16[1024,256]{1,0:T(8,128)(2,1)S(1)} %bitcast.101), kind=kOutput, calls=%fused_computation.64 | convolution fusion | flops 1144520704 | bytes 3151872 | tf_op jit(solution)/shard_map/dot_general | solution.py:54
  56.0 0.0 copy-start.7
  56.0 0.0 copy-start.8
  56.0 0.1 reduce_sum.38
  56.2 0.1 convolution_convert_fusion.1
  56.3 19.5 %all_gather.3 = bf16[256,512]{1,0:T(8,128)(2,1)S(1)} all-gather(bf16[16,512]{1,0:T(8,128)(2,1)S(1)} %convolution_convert_fusion.1), channel_id=1, replica_groups=mesh['row'=16,'col'=16] {'col'}, dimensions={0}, use_global_device_ids=true | all-gather | bytes 278528 | tf_op jit(solution)/shard_map/all_gather | solution.py:102
  75.9 0.1 copy.19
  76.0 0.1 copy.20
  76.1 0.1 convolution_convert_fusion.2
  76.2 0.1 reshape.111
  76.3 0.1 fusion.17
  76.5 0.2 fusion.108
  76.7 0.3 fusion.18
  77.0 0.1 reshape.115
  77.1 0.1 fusion.59
  77.2 0.1 broadcast_in_dim.2
  77.4 0.9 %add_convert_fusion = bf16[32,32,256]{2,1,0:T(8,128)(2,1)} fusion(f32[32,32,256]{2,1,0:T(8,128)S(1)} %bitcast.99, f32[32,32,256]{2,1,0:T(8,128)S(1)} %bitcast.100), kind=kLoop, calls=%fused_computation.74 | loop fusion | flops 524288 | bytes 2621440 | tf_op jit(solution)/shard_map/convert_element_type | solution.py:148
  (80 shorter events, 0.2 us)
Async XLA Ops:
  0.0 45.0 %copy-start = (bf16[1024,256]{1,0:T(8,128)(2,1)S(1)}, bf16[1024,256]{1,0:T(8,128)(2,1)}, u32[]{:S(2)}) copy-start(bf16[1024,256]{1,0:T(8,128)(2,1)} %param.21) | copy-start | bytes 1572868
  0.9 13.7 %collective-permute-start = (bf16[3,32,256]{2,1,0:T(8,128)(2,1)S(1)}, bf16[3,32,256]{2,1,0:T(8,128)(2,1)S(1)}, u32[]{:S(2)}, u32[]{:S(2)}) collective-permute-start(bf16[3,32,256]{2,1,0:T(8,128)(2,1)S(1)} %get-tuple-element.13), channel_id=1, source_target_pairs={{0,16},{16,32},{32,48},{48,64},{64,80},{80,96},{96,112},{112,128},... | collective-permute-start | bytes 147464 | tf_op jit(solution)/shard_map/ppermute | solution.py:16
  5.7 10.2 %collective-permute-start.1 = (bf16[3,32,256]{2,1,0:T(8,128)(2,1)S(1)}, bf16[3,32,256]{2,1,0:T(8,128)(2,1)S(1)}, u32[]{:S(2)}, u32[]{:S(2)}) collective-permute-start(bf16[3,32,256]{2,1,0:T(8,128)(2,1)S(1)} %get-tuple-element.12), channel_id=1, source_target_pairs={{16,0},{32,16},{48,32},{64,48},{80,64},{96,80},{112,96},{128,112},... | collective-permute-start | bytes 147464 | tf_op jit(solution)/shard_map/ppermute | solution.py:17
  15.9 7.1 %copy-start.1 = (bf16[35,32,256]{2,1,0:T(8,128)(2,1)}, bf16[35,32,256]{2,1,0:T(8,128)(2,1)S(1)}, u32[]{:S(2)}) copy-start(bf16[35,32,256]{2,1,0:T(8,128)(2,1)S(1)} %get-tuple-element.9) | copy-start | bytes 1720324
  15.9 7.1 %copy-start.4 = (bf16[38,32,256]{2,1,0:T(8,128)(2,1)}, bf16[38,32,256]{2,1,0:T(8,128)(2,1)S(1)}, u32[]{:S(2)}) copy-start(bf16[38,32,256]{2,1,0:T(8,128)(2,1)S(1)} %get-tuple-element.19) | copy-start | bytes 1867780
  16.8 13.0 %collective-permute-start.3 = (bf16[38,3,256]{2,1,0:T(4,128)(2,1)}, bf16[38,3,256]{2,1,0:T(4,128)(2,1)S(1)}, u32[]{:S(2)}, u32[]{:S(2)}) collective-permute-start(bf16[38,3,256]{2,1,0:T(4,128)(2,1)} %get-tuple-element.8), channel_id=1, source_target_pairs={{1,0},{2,1},{3,2},{4,3},{5,4},{6,5},{7,6},{8,7},{9,8},{10,9},{11,1... | collective-permute-start | bytes 175112 | tf_op jit(solution)/shard_map/ppermute | solution.py:17
  19.9 9.9 %collective-permute-start.2 = (bf16[38,3,256]{2,1,0:T(4,128)(2,1)}, bf16[38,3,256]{2,1,0:T(4,128)(2,1)}, u32[]{:S(2)}, u32[]{:S(2)}) collective-permute-start(bf16[38,3,256]{2,1,0:T(4,128)(2,1)} %get-tuple-element.7), channel_id=1, source_target_pairs={{0,1},{1,2},{2,3},{3,4},{4,5},{5,6},{6,7},{7,8},{8,9},{9,10},{10,1... | collective-permute-start | bytes 175112 | tf_op jit(solution)/shard_map/ppermute | solution.py:16
  26.9 2.9 %copy-start.2 = (bf16[35,32,256]{2,1,0:T(8,128)(2,1)S(1)}, bf16[35,32,256]{2,1,0:T(8,128)(2,1)}, u32[]{:S(2)}) copy-start(bf16[35,32,256]{2,1,0:T(8,128)(2,1)} %copy-done.1) | copy-start | bytes 1720324
  26.9 2.9 %copy-start.3 = (bf16[32,32,256]{2,1,0:T(8,128)(2,1)S(1)}, bf16[32,32,256]{2,1,0:T(8,128)(2,1)}, u32[]{:S(2)}) copy-start(bf16[32,32,256]{2,1,0:T(8,128)(2,1)} %param.14) | copy-start | bytes 1572868
  26.9 2.9 %copy-start.5 = (bf16[38,32,256]{2,1,0:T(8,128)(2,1)S(1)}, bf16[38,32,256]{2,1,0:T(8,128)(2,1)}, u32[]{:S(2)}) copy-start(bf16[38,32,256]{2,1,0:T(8,128)(2,1)} %copy-done.4) | copy-start | bytes 1867780
  26.9 2.9 %copy-start.9 = (f32[1,1,256]{2,1,0:T(1,128)S(1)}, f32[1,1,256]{2,1,0:T(1,128)}, u32[]{:S(2)}) copy-start(f32[1,1,256]{2,1,0:T(1,128)} %get-tuple-element.25) | copy-start | bytes 3076
  26.9 2.9 %copy-start.10 = (f32[1,1,256]{2,1,0:T(1,128)S(1)}, f32[1,1,256]{2,1,0:T(1,128)}, u32[]{:S(2)}) copy-start(f32[1,1,256]{2,1,0:T(1,128)} %get-tuple-element.26) | copy-start | bytes 3076
  26.9 2.9 %copy-start.11 = (f32[1,1,256]{2,1,0:T(1,128)S(1)}, f32[1,1,256]{2,1,0:T(1,128)}, u32[]{:S(2)}) copy-start(f32[1,1,256]{2,1,0:T(1,128)} %get-tuple-element.27) | copy-start | bytes 3076
  26.9 2.9 %copy-start.12 = (f32[1,1,256]{2,1,0:T(1,128)S(1)}, f32[1,1,256]{2,1,0:T(1,128)}, u32[]{:S(2)}) copy-start(f32[1,1,256]{2,1,0:T(1,128)} %get-tuple-element.28) | copy-start | bytes 3076
  27.0 2.9 %copy-start.13 = (f32[1,1,256]{2,1,0:T(1,128)S(1)}, f32[1,1,256]{2,1,0:T(1,128)}, u32[]{:S(2)}) copy-start(f32[1,1,256]{2,1,0:T(1,128)} %get-tuple-element.29) | copy-start | bytes 3076
  27.0 2.9 %copy-start.14 = (f32[1,1,256]{2,1,0:T(1,128)S(1)}, f32[1,1,256]{2,1,0:T(1,128)}, u32[]{:S(2)}) copy-start(f32[1,1,256]{2,1,0:T(1,128)} %get-tuple-element.30) | copy-start | bytes 3076
  27.0 2.9 %copy-start.15 = (f32[1,1,256]{2,1,0:T(1,128)S(1)}, f32[1,1,256]{2,1,0:T(1,128)}, u32[]{:S(2)}) copy-start(f32[1,1,256]{2,1,0:T(1,128)} %get-tuple-element.31) | copy-start | bytes 3076
  27.0 2.9 %copy-start.16 = (f32[1,1,256]{2,1,0:T(1,128)S(1)}, f32[1,1,256]{2,1,0:T(1,128)}, u32[]{:S(2)}) copy-start(f32[1,1,256]{2,1,0:T(1,128)} %get-tuple-element.32) | copy-start | bytes 3076
  27.0 2.9 %copy-start.17 = (f32[1,1,256]{2,1,0:T(1,128)S(1)}, f32[1,1,256]{2,1,0:T(1,128)}, u32[]{:S(2)}) copy-start(f32[1,1,256]{2,1,0:T(1,128)} %get-tuple-element.33) | copy-start | bytes 3076
  27.0 2.9 %copy-start.18 = (f32[1,1,256]{2,1,0:T(1,128)S(1)}, f32[1,1,256]{2,1,0:T(1,128)}, u32[]{:S(2)}) copy-start(f32[1,1,256]{2,1,0:T(1,128)} %get-tuple-element.34) | copy-start | bytes 3076
  27.0 2.9 %copy-start.19 = (f32[1,1,256]{2,1,0:T(1,128)S(1)}, f32[1,1,256]{2,1,0:T(1,128)}, u32[]{:S(2)}) copy-start(f32[1,1,256]{2,1,0:T(1,128)} %get-tuple-element.35) | copy-start | bytes 3076
  27.0 2.9 %copy-start.20 = (f32[1,1,256]{2,1,0:T(1,128)S(1)}, f32[1,1,256]{2,1,0:T(1,128)}, u32[]{:S(2)}) copy-start(f32[1,1,256]{2,1,0:T(1,128)} %get-tuple-element.36) | copy-start | bytes 3076
  27.0 2.9 %copy-start.21 = (f32[1,1,256]{2,1,0:T(1,128)S(1)}, f32[1,1,256]{2,1,0:T(1,128)}, u32[]{:S(2)}) copy-start(f32[1,1,256]{2,1,0:T(1,128)} %get-tuple-element.37) | copy-start | bytes 3076
  27.0 2.9 %copy-start.22 = (f32[1,1,256]{2,1,0:T(1,128)S(1)}, f32[1,1,256]{2,1,0:T(1,128)}, u32[]{:S(2)}) copy-start(f32[1,1,256]{2,1,0:T(1,128)} %get-tuple-element.38) | copy-start | bytes 3076
  27.1 2.9 %copy-start.23 = (f32[1,1,256]{2,1,0:T(1,128)S(1)}, f32[1,1,256]{2,1,0:T(1,128)}, u32[]{:S(2)}) copy-start(f32[1,1,256]{2,1,0:T(1,128)} %get-tuple-element.39) | copy-start | bytes 3076
  27.1 2.9 %copy-start.24 = (f32[1,1,256]{2,1,0:T(1,128)S(1)}, f32[1,1,256]{2,1,0:T(1,128)}, u32[]{:S(2)}) copy-start(f32[1,1,256]{2,1,0:T(1,128)} %get-tuple-element.40) | copy-start | bytes 3076
  27.1 2.9 %copy-start.25 = (f32[1,1,256]{2,1,0:T(1,128)S(1)}, f32[1,1,256]{2,1,0:T(1,128)}, u32[]{:S(2)}) copy-start(f32[1,1,256]{2,1,0:T(1,128)} %get-tuple-element.41) | copy-start | bytes 3076
  27.1 2.9 %copy-start.26 = (f32[1,1,256]{2,1,0:T(1,128)S(1)}, f32[1,1,256]{2,1,0:T(1,128)}, u32[]{:S(2)}) copy-start(f32[1,1,256]{2,1,0:T(1,128)} %get-tuple-element.42) | copy-start | bytes 3076
  27.1 2.9 %copy-start.27 = (f32[1,1,256]{2,1,0:T(1,128)S(1)}, f32[1,1,256]{2,1,0:T(1,128)}, u32[]{:S(2)}) copy-start(f32[1,1,256]{2,1,0:T(1,128)} %get-tuple-element.43) | copy-start | bytes 3076
  27.1 2.9 %copy-start.28 = (f32[1,1,256]{2,1,0:T(1,128)S(1)}, f32[1,1,256]{2,1,0:T(1,128)}, u32[]{:S(2)}) copy-start(f32[1,1,256]{2,1,0:T(1,128)} %get-tuple-element.44) | copy-start | bytes 3076
  27.1 2.9 %copy-start.29 = (f32[1,1,256]{2,1,0:T(1,128)S(1)}, f32[1,1,256]{2,1,0:T(1,128)}, u32[]{:S(2)}) copy-start(f32[1,1,256]{2,1,0:T(1,128)} %get-tuple-element.45) | copy-start | bytes 3076
  27.1 2.9 %copy-start.30 = (f32[1,1,256]{2,1,0:T(1,128)S(1)}, f32[1,1,256]{2,1,0:T(1,128)}, u32[]{:S(2)}) copy-start(f32[1,1,256]{2,1,0:T(1,128)} %get-tuple-element.46) | copy-start | bytes 3076
  27.1 2.9 %copy-start.31 = (f32[1,1,256]{2,1,0:T(1,128)S(1)}, f32[1,1,256]{2,1,0:T(1,128)}, u32[]{:S(2)}) copy-start(f32[1,1,256]{2,1,0:T(1,128)} %get-tuple-element.47) | copy-start | bytes 3076
  27.1 2.9 %copy-start.32 = (f32[1,1,256]{2,1,0:T(1,128)S(1)}, f32[1,1,256]{2,1,0:T(1,128)}, u32[]{:S(2)}) copy-start(f32[1,1,256]{2,1,0:T(1,128)} %get-tuple-element.48) | copy-start | bytes 3076
  27.2 2.9 %copy-start.33 = (f32[1,1,256]{2,1,0:T(1,128)S(1)}, f32[1,1,256]{2,1,0:T(1,128)}, u32[]{:S(2)}) copy-start(f32[1,1,256]{2,1,0:T(1,128)} %get-tuple-element.49) | copy-start | bytes 3076
  27.2 2.9 %copy-start.34 = (f32[1,1,256]{2,1,0:T(1,128)S(1)}, f32[1,1,256]{2,1,0:T(1,128)}, u32[]{:S(2)}) copy-start(f32[1,1,256]{2,1,0:T(1,128)} %get-tuple-element.50) | copy-start | bytes 3076
  27.2 2.9 %copy-start.35 = (f32[1,1,256]{2,1,0:T(1,128)S(1)}, f32[1,1,256]{2,1,0:T(1,128)}, u32[]{:S(2)}) copy-start(f32[1,1,256]{2,1,0:T(1,128)} %get-tuple-element.51) | copy-start | bytes 3076
  27.2 2.9 %copy-start.36 = (f32[1,1,256]{2,1,0:T(1,128)S(1)}, f32[1,1,256]{2,1,0:T(1,128)}, u32[]{:S(2)}) copy-start(f32[1,1,256]{2,1,0:T(1,128)} %get-tuple-element.52) | copy-start | bytes 3076
  27.2 2.9 %copy-start.37 = (f32[1,1,256]{2,1,0:T(1,128)S(1)}, f32[1,1,256]{2,1,0:T(1,128)}, u32[]{:S(2)}) copy-start(f32[1,1,256]{2,1,0:T(1,128)} %get-tuple-element.53) | copy-start | bytes 3076
  27.2 2.9 %copy-start.38 = (f32[1,1,256]{2,1,0:T(1,128)S(1)}, f32[1,1,256]{2,1,0:T(1,128)}, u32[]{:S(2)}) copy-start(f32[1,1,256]{2,1,0:T(1,128)} %get-tuple-element.54) | copy-start | bytes 3076
  27.2 2.9 %copy-start.39 = (f32[1,1,256]{2,1,0:T(1,128)S(1)}, f32[1,1,256]{2,1,0:T(1,128)}, u32[]{:S(2)}) copy-start(f32[1,1,256]{2,1,0:T(1,128)} %get-tuple-element.55) | copy-start | bytes 3076
  27.2 2.9 %copy-start.40 = (f32[1,1,256]{2,1,0:T(1,128)S(1)}, f32[1,1,256]{2,1,0:T(1,128)}, u32[]{:S(2)}) copy-start(f32[1,1,256]{2,1,0:T(1,128)} %get-tuple-element.56) | copy-start | bytes 3076
  27.2 2.9 %copy-start.41 = (f32[1,1,256]{2,1,0:T(1,128)S(1)}, f32[1,1,256]{2,1,0:T(1,128)}, u32[]{:S(2)}) copy-start(f32[1,1,256]{2,1,0:T(1,128)} %get-tuple-element.57) | copy-start | bytes 3076
  27.2 2.9 %copy-start.42 = (f32[1,1,256]{2,1,0:T(1,128)S(1)}, f32[1,1,256]{2,1,0:T(1,128)}, u32[]{:S(2)}) copy-start(f32[1,1,256]{2,1,0:T(1,128)} %get-tuple-element.58) | copy-start | bytes 3076
  27.3 2.9 %copy-start.43 = (f32[1,1,256]{2,1,0:T(1,128)S(1)}, f32[1,1,256]{2,1,0:T(1,128)}, u32[]{:S(2)}) copy-start(f32[1,1,256]{2,1,0:T(1,128)} %get-tuple-element.59) | copy-start | bytes 3076
  27.3 2.9 %copy-start.44 = (f32[1,1,256]{2,1,0:T(1,128)S(1)}, f32[1,1,256]{2,1,0:T(1,128)}, u32[]{:S(2)}) copy-start(f32[1,1,256]{2,1,0:T(1,128)} %get-tuple-element.60) | copy-start | bytes 3076
  43.5 1.5 %copy-start.45 = (f32[1024]{0:T(1024)S(1)}, f32[1024]{0:T(1024)}, u32[]{:S(2)}) copy-start(f32[1024]{0:T(1024)} %param.20) | copy-start | bytes 12292
  43.6 1.5 %copy-start.46 = (f32[256]{0:T(256)S(1)}, f32[256]{0:T(256)}, u32[]{:S(2)}) copy-start(f32[256]{0:T(256)} %param.22) | copy-start | bytes 3076
  43.6 1.5 %copy-start.47 = (f32[256]{0:T(256)S(1)}, f32[256]{0:T(256)}, u32[]{:S(2)}) copy-start(f32[256]{0:T(256)} %param.23) | copy-start | bytes 3076
  45.1 11.1 %copy-start.6 = (bf16[256,512]{1,0:T(8,128)(2,1)S(1)}, bf16[256,512]{1,0:T(8,128)(2,1)}, u32[]{:S(2)}) copy-start(bf16[256,512]{1,0:T(8,128)(2,1)} %param.25) | copy-start | bytes 786436
  56.0 20.1 %copy-start.7 = (bf16[256,256]{1,0:T(8,128)(2,1)S(1)}, bf16[256,256]{1,0:T(8,128)(2,1)}, u32[]{:S(2)}) copy-start(bf16[256,256]{1,0:T(8,128)(2,1)} %param.24) | copy-start | bytes 393220
  56.0 21.1 %copy-start.8 = (bf16[256,256]{1,0:T(8,128)(2,1)S(1)}, bf16[256,256]{1,0:T(8,128)(2,1)}, u32[]{:S(2)}) copy-start(bf16[256,256]{1,0:T(8,128)(2,1)} %param.27) | copy-start | bytes 393220
where the time goes:
time: 79.1 us; the launch traced here: 78.3 us
  other arithmetic  20.9 us (26%)
  blocking collectives  19.5 us (25%)
  starting transfers between devices  15.1 us (19%)
  matrix products  13.2 us (17%)
  local copies, waits for them, and re-layouts  8.61 us (11%)
  between operations  0.98 us (1%)
    all_gather x1, blocking collectives, shards(): band_keyval = lax.all_gather(keyval, 'col', axis=0, tiled=True)  19.5 us
    reduce_sum x1, other arithmetic, block_pass(): average = jnp.mean(convolved, axis=-1, keepdims=True)  13.4 us
    dot_general x1, matrix products, block_pass(): jnp.dot(hidden, w_reduce, preferred_element_type=jnp.float32) + b_reduce  10.9 us
    ppermute x2, starting transfers between devices, padded_2(): before = lax.ppermute(last, axis, up)  7.91 us
    ppermute x2, starting transfers between devices, padded_2(): after = lax.ppermute(leading, axis, down)  7.2 us
    mul x3, other arithmetic, block_pass(): padded[tap_row:tap_row + tile_rows, tap_col:tap_col + tile_cols]  4.79 us
    reshape x1, local copies, waits for them, and re-layouts, shards(): jnp.transpose(both_picked, (0, 1, 2, 4, 3, 5))  2.47 us
    transpose x1, local copies, waits for them, and re-layouts, shards(): jnp.transpose(both_picked, (0, 1, 2, 4, 3, 5))  1.76 us
  transfers between devices with their start and end apart: 4, of which 0 were waited for; matrix products, arithmetic and copies ran while one was open for 16% of the time, Pallas kernels for 0%

commit v1 on v0

--- a/solution.py
+++ b/solution.py
@@ -4,6 +4,11 @@
 from jax.sharding import PartitionSpec as P
 
 HEADS = 8
+
+
+def exchange_gather(value, axis, dim):
+    outgoing = jnp.stack([value] * lax.axis_size(axis))
+    return jnp.concatenate(lax.all_to_all(outgoing, axis, 0, 0), axis=dim)
 
 
 def padded_2(array, sides, width):
@@ -99,7 +104,7 @@
     pooled = pooled.astype(jnp.bfloat16).reshape(local_count, channels)
     queries = jnp.dot(pooled, w_query, preferred_element_type=jnp.float32).astype(jnp.bfloat16)
     keyval = jnp.dot(pooled, w_keyval, preferred_element_type=jnp.float32).astype(jnp.bfloat16)
-    band_keyval = lax.all_gather(keyval, "col", axis=0, tiled=True)
+    band_keyval = exchange_gather(keyval, "col", 0)
     columns = lax.axis_size("col")
     position = lax.axis_index("col")
     span_cols = region_side * columns

time: 79.1 us -> 63.4 us (0.80)
  blocking collectives: 19.5 us -> 0 us
  starting transfers between devices: 15.1 us -> 22 us
  other arithmetic: 20.9 us -> 15.7 us
  waiting for transfers between devices: 0.01 us -> 3.49 us
    all_gather x1 -> x0, blocking collectives: 19.5 us -> none  [shards(): band_keyval = lax.all_gather(keyval, 'col', axis=0, tiled=True)]
    all_to_all x0 -> x1, starting transfers between devices: none -> 6.85 us  [exchange_gather(): return jnp.concatenate(lax.all_to_all(outgoing, axis, 0, 0), axis=dim)]
    reduce_sum x1, other arithmetic: 13.4 us -> 10.7 us  [block_pass(): average = jnp.mean(convolved, axis=-1, keepdims=True)]
    all_to_all x0 -> x1, waiting for transfers between devices: none -> 2.13 us  [exchange_gather(): return jnp.concatenate(lax.all_to_all(outgoing, axis, 0, 0), axis=dim)]
    mul x3, other arithmetic: 4.79 us -> 2.89 us  [block_pass(): padded[tap_row:tap_row + tile_rows, tap_col:tap_col + tile_cols]]
    ppermute x2, waiting for transfers between devices: 0.01 us -> 1.29 us  [padded_2(): before = lax.ppermute(last, axis, up)]
  transfers between devices with their start and end apart: 4 -> 5, of which waited for: 0 -> 3; matrix products, arithmetic and copies ran while one was open for 16% -> 17% of each run, Pallas kernels for 0% -> 0%
where the time goes in v1:
time: 63.4 us; the launch traced here: 62.9 us
  starting transfers between devices  22 us (35%)
  other arithmetic  15.7 us (25%)
  matrix products  13.2 us (21%)
  local copies, waits for them, and re-layouts  8.18 us (13%)
  waiting for transfers between devices  3.49 us (6%)
    dot_general x1, matrix products, block_pass(): jnp.dot(hidden, w_reduce, preferred_element_type=jnp.float32) + b_reduce  10.9 us
    reduce_sum x1, other arithmetic, block_pass(): average = jnp.mean(convolved, axis=-1, keepdims=True)  10.7 us
    ppermute x2, starting transfers between devices, padded_2(): before = lax.ppermute(last, axis, up)  7.91 us
    ppermute x2, starting transfers between devices, padded_2(): after = lax.ppermute(leading, axis, down)  7.22 us
    all_to_all x1, starting transfers between devices, exchange_gather(): return jnp.concatenate(lax.all_to_all(outgoing, axis, 0, 0), axis=dim)  6.85 us
    mul x3, other arithmetic, block_pass(): padded[tap_row:tap_row + tile_rows, tap_col:tap_col + tile_cols]  2.89 us
    reshape x1, local copies, waits for them, and re-layouts, shards(): jnp.transpose(both_picked, (0, 1, 2, 4, 3, 5))  2.21 us
    all_to_all x1, waiting for transfers between devices, exchange_gather(): return jnp.concatenate(lax.all_to_all(outgoing, axis, 0, 0), axis=dim)  2.13 us
  transfers between devices with their start and end apart: 5, of which 3 were waited for; matrix products, arithmetic and copies ran while one was open for 17% of the time, Pallas kernels for 0%

profile of v1, /device:TPU:129, one launch (start us, length us, event | category | flops | bytes accessed | tf_op | source)
XLA Modules:
  0.0 62.9 jit_solution(1740060132887368057)
XLA Ops:
  0.0 0.0 copy-start
  0.0 0.0 copy-start.3
  0.0 0.0 copy-start.7
  0.0 0.9 %fusion.106 = (bf16[3,32,256]{2,1,0:T(8,128)(2,1)S(1)}, bf16[3,32,256]{2,1,0:T(8,128)(2,1)S(1)}) fusion(bf16[32,32,256]{2,1,0:T(8,128)(2,1)} %param.14), kind=kLoop, calls=%fused_computation.266 | loop fusion | bytes 196608 | tf_op jit(solution)/shard_map/slice | solution.py:20
  0.9 4.8 %collective-permute-start = (bf16[3,32,256]{2,1,0:T(8,128)(2,1)S(1)}, bf16[3,32,256]{2,1,0:T(8,128)(2,1)S(1)}, u32[]{:S(2)}, u32[]{:S(2)}) collective-permute-start(bf16[3,32,256]{2,1,0:T(8,128)(2,1)S(1)} %get-tuple-element.13), channel_id=1, source_target_pairs={{0,16},{16,32},{32,48},{48,64},{64,80},{80,96},{96,112},{112,128},... | collective-permute-start | bytes 147464 | tf_op jit(solution)/shard_map/ppermute | solution.py:21
  5.7 4.1 %collective-permute-start.1 = (bf16[3,32,256]{2,1,0:T(8,128)(2,1)S(1)}, bf16[3,32,256]{2,1,0:T(8,128)(2,1)S(1)}, u32[]{:S(2)}, u32[]{:S(2)}) collective-permute-start(bf16[3,32,256]{2,1,0:T(8,128)(2,1)S(1)} %get-tuple-element.12), channel_id=1, source_target_pairs={{16,0},{32,16},{48,32},{64,48},{80,64},{96,80},{112,96},{128,112},... | collective-permute-start | bytes 147464 | tf_op jit(solution)/shard_map/ppermute | solution.py:22
  9.8 0.9 %slice_convert_fusion.46 = (f32[1,1,256]{2,1,0:T(1,128)S(1)}, f32[1,1,256]{2,1,0:T(1,128)S(1)}, f32[1,1,256]{2,1,0:T(1,128)S(1)}, f32[1,1,256]{2,1,0:T(1,128)S(1...) fusion(bf16[7,7,256]{2,1,0:T(8,128)(2,1)} %param.15), kind=kLoop, calls=%fused_computation.229 | loop fusion | flops 2816 | bytes 16896 | tf_op jit(solution)/shard_map/mul | solution.py:44
  10.7 1.0 %slice_convert_fusion.48 = (f32[1,1,256]{2,1,0:T(1,128)S(1)}, f32[1,1,256]{2,1,0:T(1,128)S(1)}, f32[1,1,256]{2,1,0:T(1,128)S(1)}, f32[1,1,256]{2,1,0:T(1,128)S(1...) fusion(bf16[7,7,256]{2,1,0:T(8,128)(2,1)} %param.15), kind=kLoop, calls=%fused_computation.231 | loop fusion | flops 4864 | bytes 29184 | tf_op jit(solution)/shard_map/mul | solution.py:44
  11.7 1.0 %slice_convert_fusion.47 = (f32[1,1,256]{2,1,0:T(1,128)S(1)}, f32[1,1,256]{2,1,0:T(1,128)S(1)}, f32[1,1,256]{2,1,0:T(1,128)S(1)}, f32[1,1,256]{2,1,0:T(1,128)S(1...) fusion(bf16[7,7,256]{2,1,0:T(8,128)(2,1)} %param.15), kind=kLoop, calls=%fused_computation.230 | loop fusion | flops 4864 | bytes 29184 | tf_op jit(solution)/shard_map/mul | solution.py:44
  12.7 1.0 %fusion.67 = f32[4,4,8,127]{3,1,2,0:T(4,128)S(1)} fusion(f32[8,7,127,1]{2,0,1,3:T(8,128)} %bitcast.107, s32[4,4]{1,0:T(4,128)S(1)} %subtract_add_fusion), kind=kOutput, calls=%fused_computation.165 | convolution fusion | flops 1365616 | bytes 93536 | tf_op jit(solution)/shard_map/rso,hoc->hrsc/dot_general | solution.py:117
  13.8 0.0 collective-permute-done
  13.8 1.2 %constant_dynamic-update-slice_fusion.3 = (bf16[35,32,256]{2,1,0:T(8,128)(2,1)S(1)}, bf16[38,32,256]{2,1,0:T(8,128)(2,1)S(1)}, bf16[35,32,256]{2,1,0:T(8,128)(2,1)S(1)}) fusion(bf16[35,32,256]{2,1,0:T(8,128)(2,1)S(1)} %get-tuple-element.16, bf16[32,32,256]{2,1,0:T(8,128)(2,1)} %param.14, bf16[38,32,256]{2,1,0:T(8,128)(2,1)S(1)} %get-tuple-element.17), kind=kLoop, calls=%fused_computation.171 | loop fusion | bytes 2097152 | tf_op jit(solution)/shard_map/concatenate | solution.py:23
  15.0 0.0 collective-permute-done.1
  15.0 0.1 fusion.105
  15.1 3.1 %collective-permute-start.3 = (bf16[38,3,256]{2,1,0:T(4,128)(2,1)S(1)}, bf16[38,3,256]{2,1,0:T(4,128)(2,1)S(1)}, u32[]{:S(2)}, u32[]{:S(2)}) collective-permute-start(bf16[38,3,256]{2,1,0:T(4,128)(2,1)S(1)} %get-tuple-element.8), channel_id=1, source_target_pairs={{1,0},{2,1},{3,2},{4,3},{5,4},{6,5},{7,6},{8,7},{9,8},{10,9},{11,1... | collective-permute-start | bytes 175112 | tf_op jit(solution)/shard_map/ppermute | solution.py:22
  18.3 3.1 %collective-permute-start.2 = (bf16[38,3,256]{2,1,0:T(4,128)(2,1)S(1)}, bf16[38,3,256]{2,1,0:T(4,128)(2,1)S(1)}, u32[]{:S(2)}, u32[]{:S(2)}) collective-permute-start(bf16[38,3,256]{2,1,0:T(4,128)(2,1)S(1)} %get-tuple-element.7), channel_id=1, source_target_pairs={{0,1},{1,2},{2,3},{3,4},{4,5},{5,6},{6,7},{7,8},{8,9},{9,10},{10,1... | collective-permute-start | bytes 175112 | tf_op jit(solution)/shard_map/ppermute | solution.py:21
  21.4 0.1 subtract_add_fusion.1
  21.5 0.1 collective-permute-done.3
  21.5 1.3 %collective-permute-done.2 = bf16[38,3,256]{2,1,0:T(4,128)(2,1)S(1)} collective-permute-done((bf16[38,3,256]{2,1,0:T(4,128)(2,1)S(1)}, bf16[38,3,256]{2,1,0:T(4,128)(2,1)S(1)}, u32[]{:S(2)}, u32[]{:S(2)}) %collective-permute-start.2) | collective-permute-done | bytes 58400 | tf_op jit(solution)/shard_map/ppermute | solution.py:21
  22.8 0.0 copy-done.3
  22.8 0.0 copy-done.7
  22.8 0.0 copy-start.8
  22.8 0.0 copy-start.9
  22.8 10.7 %fusion.104 = (f32[32,32]{1,0:T(8,128)S(1)}, f32[32,32,256]{2,1,0:T(8,128)S(1)}) fusion(f32[256]{0:T(256)S(1)} %copy-done.7, f32[256]{0:T(256)S(1)} %bitcast.117, bf16[38,3,256]{2,1,0:T(4,128)(2,1)S(1)} %collective-permute-done.3, bf16[38,32,256]{2,1,0:T(8,128)(2,1)S(1)} %get-tuple-element.19, f32[256]{0:T(256)S(1)} %bitcast.118, f32[256]{0:T(256)S(1)} %bitcast.120, ...), kind=kLoop, calls=%fused_computation.264 | loop fusion | flops 71826432 | bytes 5513216 | tf_op jit(solution)/shard_map/reduce_sum | solution.py:48
  33.5 0.0 copy-start.10
  33.6 0.0 copy-start.11
  33.6 0.0 copy-start.12
  33.6 0.4 multiply_reduce_fusion
  34.0 0.0 copy-done.8
  34.0 0.0 copy-done.9
  34.0 0.3 add_convert_fusion.1
  34.4 0.0 copy-done
  34.4 0.0 copy-done.10
  34.4 0.0 copy-done.11
  34.4 0.0 copy-done.12
  34.4 0.0 copy-start.4
  34.4 10.9 %fusion.14 = f32[1024,256]{1,0:T(8,128)S(1)} fusion(bf16[1024,256]{1,0:T(8,128)(2,1)S(1)} %copy-done, bf16[1024,256]{1,0:T(8,128)(2,1)S(1)} %bitcast.104, bf16[256,1024]{1,0:T(8,128)(2,1)} %param.19, f32[1024]{0:T(1024)S(1)} %copy-done.10, f32[256]{0:T(256)S(1)} %copy-done.11, f32[256]{0:T(256)S(1)} %copy-done.12, bf16[1024,256]{1,0:T(8,128)(2,1)S(1)} %bitcast.102), kind=kOutput, calls=%fused_computation.64 | convolution fusion | flops 1144520704 | bytes 3151872 | tf_op jit(solution)/shard_map/dot_general | solution.py:59
  45.3 0.0 copy-start.1
  45.4 0.1 reduce_sum.38
  45.5 0.0 copy-done.4
  45.5 0.1 convolution_convert_fusion.1
  45.6 0.8 %stack.2 = bf16[16,16,512]{2,1,0:T(8,128)(2,1)} broadcast(bf16[16,512]{1,0:T(8,128)(2,1)S(1)} %convolution_convert_fusion.1), dimensions={1,2} | broadcast | bytes 278528 | tf_op jit(solution)/shard_map/stack | solution.py:10
  46.4 6.9 %all-to-all-start = ((bf16[16,16,512]{2,1,0:T(8,128)(2,1)}), bf16[16,16,512]{2,1,0:T(8,128)(2,1)S(1)}, u32[]{:S(2)}, u32[]{:S(2)}) async-start(bf16[16,16,512]{2,1,0:T(8,128)(2,1)} %stack.2), calls=%async_computation | async-start | bytes 524288 | tf_op jit(solution)/shard_map/all_to_all | solution.py:11
  53.2 0.0 copy-done.1
  53.2 0.4 convolution_bitcast_fusion
  53.7 0.6 copy.21
  54.3 1.7 %copy.22 = f32[8,4,4,16,4,4]{0,5,4,3,2,1:T(4,128)} copy(f32[8,4,4,16,4,4]{0,5,3,4,2,1:T(4,128)S(1)} %bitcast.97) | data formatting | bytes 262144 | tf_op jit(solution)/shard_map/transpose | solution.py:130
  56.0 2.2 %copy.23 = f32[8,16,256]{2,1,0:T(8,128)S(1)} copy(f32[8,16,256]{0,2,1:T(8,128)} %bitcast.98) | data formatting | bytes 262144 | tf_op jit(solution)/shard_map/reshape | solution.py:130
  58.2 0.0 copy-done.5
  58.3 0.0 copy-start.2
  58.3 0.1 convolution_convert_fusion.2
  58.4 0.1 reshape.117
  58.5 2.1 %all-to-all-done = bf16[16,16,512]{2,1,0:T(8,128)(2,1)S(1)} async-done(((bf16[16,16,512]{2,1,0:T(8,128)(2,1)}), bf16[16,16,512]{2,1,0:T(8,128)(2,1)S(1)}, u32[]{:S(2)}, u32[]{:S(2)}) %all-to-all-start) | async-done | bytes 262176 | tf_op jit(solution)/shard_map/all_to_all | solution.py:11
  60.7 0.1 copy.18
  60.8 0.1 copy.19
  60.9 0.1 fusion.17
  61.0 0.2 fusion.108
  61.2 0.3 fusion.18
  61.5 0.1 reshape.121
  61.6 0.0 copy-done.6
  61.6 0.1 fusion.59
  61.8 0.1 broadcast_in_dim.2
  61.9 0.0 copy-done.2
  61.9 1.0 %add_convert_fusion = bf16[32,32,256]{2,1,0:T(8,128)(2,1)} fusion(f32[32,32,256]{2,1,0:T(8,128)S(1)} %bitcast.100, f32[32,32,256]{2,1,0:T(8,128)S(1)} %bitcast.101), kind=kLoop, calls=%fused_computation.74 | loop fusion | flops 524288 | bytes 2621440 | tf_op jit(solution)/shard_map/convert_element_type | solution.py:153
  (12 shorter events, 0.1 us)
Async XLA Ops:
  0.0 34.4 %copy-start = (bf16[1024,256]{1,0:T(8,128)(2,1)S(1)}, bf16[1024,256]{1,0:T(8,128)(2,1)}, u32[]{:S(2)}) copy-start(bf16[1024,256]{1,0:T(8,128)(2,1)} %param.21) | copy-start | bytes 1572868
  0.0 22.8 %copy-start.3 = (bf16[32,32,256]{2,1,0:T(8,128)(2,1)S(1)}, bf16[32,32,256]{2,1,0:T(8,128)(2,1)}, u32[]{:S(2)}) copy-start(bf16[32,32,256]{2,1,0:T(8,128)(2,1)} %param.14) | copy-start | bytes 1572868
  0.0 22.8 %copy-start.7 = (f32[256]{0:T(256)S(1)}, f32[256]{0:T(256)}, u32[]{:S(2)}) copy-start(f32[256]{0:T(256)} %param.16) | copy-start | bytes 3076
  0.9 12.8 %collective-permute-start = (bf16[3,32,256]{2,1,0:T(8,128)(2,1)S(1)}, bf16[3,32,256]{2,1,0:T(8,128)(2,1)S(1)}, u32[]{:S(2)}, u32[]{:S(2)}) collective-permute-start(bf16[3,32,256]{2,1,0:T(8,128)(2,1)S(1)} %get-tuple-element.13), channel_id=1, source_target_pairs={{0,16},{16,32},{32,48},{48,64},{64,80},{80,96},{96,112},{112,128},... | collective-permute-start | bytes 147464 | tf_op jit(solution)/shard_map/ppermute | solution.py:21
  5.7 9.3 %collective-permute-start.1 = (bf16[3,32,256]{2,1,0:T(8,128)(2,1)S(1)}, bf16[3,32,256]{2,1,0:T(8,128)(2,1)S(1)}, u32[]{:S(2)}, u32[]{:S(2)}) collective-permute-start(bf16[3,32,256]{2,1,0:T(8,128)(2,1)S(1)} %get-tuple-element.12), channel_id=1, source_target_pairs={{16,0},{32,16},{48,32},{64,48},{80,64},{96,80},{112,96},{128,112},... | collective-permute-start | bytes 147464 | tf_op jit(solution)/shard_map/ppermute | solution.py:22
  15.1 6.4 %collective-permute-start.3 = (bf16[38,3,256]{2,1,0:T(4,128)(2,1)S(1)}, bf16[38,3,256]{2,1,0:T(4,128)(2,1)S(1)}, u32[]{:S(2)}, u32[]{:S(2)}) collective-permute-start(bf16[38,3,256]{2,1,0:T(4,128)(2,1)S(1)} %get-tuple-element.8), channel_id=1, source_target_pairs={{1,0},{2,1},{3,2},{4,3},{5,4},{6,5},{7,6},{8,7},{9,8},{10,9},{11,1... | collective-permute-start | bytes 175112 | tf_op jit(solution)/shard_map/ppermute | solution.py:22
  18.3 4.5 %collective-permute-start.2 = (bf16[38,3,256]{2,1,0:T(4,128)(2,1)S(1)}, bf16[38,3,256]{2,1,0:T(4,128)(2,1)S(1)}, u32[]{:S(2)}, u32[]{:S(2)}) collective-permute-start(bf16[38,3,256]{2,1,0:T(4,128)(2,1)S(1)} %get-tuple-element.7), channel_id=1, source_target_pairs={{0,1},{1,2},{2,3},{3,4},{4,5},{5,6},{6,7},{7,8},{8,9},{9,10},{10,1... | collective-permute-start | bytes 175112 | tf_op jit(solution)/shard_map/ppermute | solution.py:21
  22.8 11.2 %copy-start.8 = (f32[256]{0:T(256)S(1)}, f32[256]{0:T(256)}, u32[]{:S(2)}) copy-start(f32[256]{0:T(256)} %param.18) | copy-start | bytes 3076
  22.8 11.2 %copy-start.9 = (f32[256]{0:T(256)S(1)}, f32[256]{0:T(256)}, u32[]{:S(2)}) copy-start(f32[256]{0:T(256)} %param.17) | copy-start | bytes 3076
  33.5 0.8 %copy-start.10 = (f32[1024]{0:T(1024)S(1)}, f32[1024]{0:T(1024)}, u32[]{:S(2)}) copy-start(f32[1024]{0:T(1024)} %param.20) | copy-start | bytes 12292
  33.6 0.8 %copy-start.11 = (f32[256]{0:T(256)S(1)}, f32[256]{0:T(256)}, u32[]{:S(2)}) copy-start(f32[256]{0:T(256)} %param.22) | copy-start | bytes 3076
  33.6 0.8 %copy-start.12 = (f32[256]{0:T(256)S(1)}, f32[256]{0:T(256)}, u32[]{:S(2)}) copy-start(f32[256]{0:T(256)} %param.23) | copy-start | bytes 3076
  34.4 11.1 %copy-start.4 = (bf16[256,512]{1,0:T(8,128)(2,1)S(1)}, bf16[256,512]{1,0:T(8,128)(2,1)}, u32[]{:S(2)}) copy-start(bf16[256,512]{1,0:T(8,128)(2,1)} %param.25) | copy-start | bytes 786436
  45.3 7.9 %copy-start.1 = (f32[1024,256]{1,0:T(8,128)}, f32[1024,256]{1,0:T(8,128)S(1)}, u32[]{:S(2)}) copy-start(f32[1024,256]{1,0:T(8,128)S(1)} %fusion.14) | copy-start | bytes 3145732
  46.4 14.3 %all-to-all-start = ((bf16[16,16,512]{2,1,0:T(8,128)(2,1)}), bf16[16,16,512]{2,1,0:T(8,128)(2,1)S(1)}, u32[]{:S(2)}, u32[]{:S(2)}) async-start(bf16[16,16,512]{2,1,0:T(8,128)(2,1)} %stack.2), calls=%async_computation | async-start | bytes 524288 | tf_op jit(solution)/shard_map/all_to_all | solution.py:11
  56.0 2.2 %copy-start.5 = (bf16[256,256]{1,0:T(8,128)(2,1)S(1)}, bf16[256,256]{1,0:T(8,128)(2,1)}, u32[]{:S(2)}) copy-start(bf16[256,256]{1,0:T(8,128)(2,1)} %param.24) | copy-start | bytes 393220
  56.0 5.6 %copy-start.6 = (bf16[256,256]{1,0:T(8,128)(2,1)S(1)}, bf16[256,256]{1,0:T(8,128)(2,1)}, u32[]{:S(2)}) copy-start(bf16[256,256]{1,0:T(8,128)(2,1)} %param.27) | copy-start | bytes 393220
  58.3 3.6 %copy-start.2 = (f32[1024,256]{1,0:T(8,128)S(1)}, f32[1024,256]{1,0:T(8,128)}, u32[]{:S(2)}) copy-start(f32[1024,256]{1,0:T(8,128)} %copy-done.1) | copy-start | bytes 3145732
